TPU v7x, 32 devices: a whole 2x2x4 slice. The times are simulated.
32 devices in a mesh: groups: 2 (over y), pairs: 4 (over z), mp: 4 (over x, core).
Axes of the slice: x: 2, y: 2, z: 4, core: 2. Of those that a mesh axis runs over, the one named last changes fastest.
Arguments:
- tokens: bfloat16 [512, 768], P(('groups', 'pairs'), 'mp'), parts along dimension 0, may hold values from -6 to 6
- pair_list: int32 [16, 2], P(('groups', 'pairs')), parts along dimension 0, may hold values from 0 to 7, as said below
- confidence: float32 [16, 64], P(('groups', 'pairs')), parts along dimension 0, may hold values from 0.1 to 10
- gain_self: float32 [768], replicated, may hold values from 0.1 to 1.9
- gain_query: float32 [768], replicated, may hold values from 0.1 to 1.9
- gain_context: float32 [768], replicated, may hold values from 0.1 to 1.9
- gain_mlp: float32 [768], replicated, may hold values from 0.1 to 1.9
- self_qkv: bfloat16 [3, 768, 768], P(None, None, 'mp'), may hold values from -1 to 1
- self_out: bfloat16 [768, 768], P('mp'), may hold values from -0.21875 to 0.21875
- cross_query: bfloat16 [768, 768], P(None, 'mp'), may hold values from -1 to 1
- cross_kv: bfloat16 [2, 768, 768], P(None, None, 'mp'), may hold values from -1 to 1
- cross_out: bfloat16 [768, 768], P('mp'), may hold values from -0.21875 to 0.21875
- mlp_up: bfloat16 [768, 3072], P(None, 'mp'), may hold values from -0.21875 to 0.21875
- mlp_down: bfloat16 [3072, 768], P('mp'), may hold values from -0.109375 to 0.109375
Outputs:
- image_features: bfloat16 [512, 768], P(('groups', 'pairs'), 'mp'), parts along dimension 0
There are 2 independent parts, one for each index of `groups`. A program takes and returns all parts, laid end to end along the dimension named above; an argument that names none is the same for every part. Nothing has to cross between parts.
Inputs may be any that keep to these rules, and one draw needn't show every extreme that they name: `pair_list`: in each block of 2 consecutive pairs the 4 images named are distinct and have distinct owners, the owner of image i being i // 2; the images of each owner are named in exactly 4 blocks; some images are named by no pair.
All inputs are finite; a program needn't handle non-finite values.
Results may differ from a plain program's by a relative error of at most 0.012.
Values may be sent and summed in bfloat16 or wider, within the bound.
No kernel may reach another device: no remote copies, remote signals or barrier semaphores. Data moves between devices by JAX's collectives and lax.ppermute only.
A program may use at most 64 MiB of HBM per device.

v0:
```python
import jax
import jax.numpy as jnp
from jax import lax
from jax.sharding import PartitionSpec as P

HEAD = 64
TOKS = 32
EPSILON = 1e-06


def layer_norm(values, gain):
    center = values - jnp.mean(values, axis=-1, keepdims=True)
    spread = jnp.mean(center * center, axis=-1, keepdims=True)
    return (center * lax.rsqrt(spread + EPSILON) * gain).astype(jnp.bfloat16)


def attend(query, keys, values, views_n):
    rows_n, width = query.shape
    heads_n = width // HEAD
    qh = query.reshape(views_n, TOKS, heads_n, HEAD)
    kh = keys.reshape(views_n, TOKS, heads_n, HEAD)
    vh = values.reshape(views_n, TOKS, heads_n, HEAD)
    scores = jnp.einsum("vqhc,vkhc->vhqk", qh, kh, preferred_element_type=jnp.float32) * HEAD ** (
        -0.5
    )
    probs = jax.nn.softmax(scores, axis=-1).astype(jnp.bfloat16)
    mixed = jnp.einsum("vhqk,vkhc->vqhc", probs, vh, preferred_element_type=jnp.float32)
    return mixed.astype(jnp.bfloat16).reshape(rows_n, width)


def swap(values, pairs):
    return lax.ppermute(values, "mp", pairs)


def mp_pairs(bit):
    n = 4
    return [(i, i ^ bit) for i in range(n)]


def mp_allreduce(term):
    if lax.axis_size("mp") != 4:
        return lax.psum(term.astype(jnp.float32), "mp")
    core = lax.axis_index("mp") % 2
    rows_n = term.shape[0]
    halves = term.reshape(2, rows_n // 2, term.shape[1])
    keep = jnp.where(core == 0, halves[0], halves[1])
    send = jnp.where(core == 0, halves[1], halves[0])
    got = swap(send, mp_pairs(1))
    chip_sum = (keep.astype(jnp.float32) + got.astype(jnp.float32)).astype(jnp.bfloat16)
    other = swap(chip_sum, mp_pairs(2))
    total = chip_sum.astype(jnp.float32) + other.astype(jnp.float32)
    rest = swap(total, mp_pairs(1))
    first = jnp.where(core == 0, total, rest)
    second = jnp.where(core == 0, rest, total)
    return jnp.concatenate([first, second], axis=0)


def mp_reduce_cols(term):
    if lax.axis_size("mp") != 4:
        full = lax.psum(term.astype(jnp.float32), "mp")
        quarter = term.shape[1] // lax.axis_size("mp")
        return lax.dynamic_slice_in_dim(full, lax.axis_index("mp") * quarter, quarter, 1)
    index = lax.axis_index("mp")
    core = index % 2
    chip = index // 2
    rows_n, width = term.shape
    parts = term.reshape(rows_n, 2, 2, width // 4)
    keep = jnp.where(core == 0, parts[:, :, 0], parts[:, :, 1])
    send = jnp.where(core == 0, parts[:, :, 1], parts[:, :, 0])
    got = swap(send, mp_pairs(1))
    both = keep.astype(jnp.float32) + got.astype(jnp.float32)
    mine = jnp.where(chip == 0, both[:, 0], both[:, 1])
    theirs = jnp.where(chip == 0, both[:, 1], both[:, 0])
    other = swap(theirs, mp_pairs(2))
    return mine + other


def mp_gather_cols(part):
    if lax.axis_size("mp") != 4:
        return lax.all_gather(part, "mp", axis=2, tiled=True)
    index = lax.axis_index("mp")
    core = index % 2
    chip = index // 2
    got = swap(part, mp_pairs(1))
    pair = jnp.where(
        core == 0, jnp.concatenate([part, got], axis=2), jnp.concatenate([got, part], axis=2)
    )
    other = swap(pair, mp_pairs(2))
    return jnp.where(
        chip == 0, jnp.concatenate([pair, other], axis=2), jnp.concatenate([other, pair], axis=2)
    )


def per_device(
    tokens,
    pair_list,
    confidence,
    gain_self,
    gain_query,
    gain_context,
    gain_mlp,
    self_qkv,
    self_out,
    cross_query,
    cross_kv,
    cross_out,
    mlp_up,
    mlp_down,
):
    quarter = tokens.shape[1]
    img_dev = tokens.shape[0] // TOKS
    pair_dev = pair_list.shape[0]
    views_n = 2 * pair_dev
    owners_n = lax.axis_size("pairs")
    every = lax.all_gather(tokens, "pairs", axis=0, tiled=True).reshape(
        owners_n * img_dev, TOKS, quarter
    )
    ids = pair_list.reshape(views_n)
    slices = jnp.take(every, ids, axis=0)
    start = mp_gather_cols(slices)
    width = start.shape[2]
    rows_n = views_n * TOKS
    flipped = start.reshape(pair_dev, 2, TOKS, width)
    flipped = jnp.concatenate([flipped[:, 1:], flipped[:, :1]], axis=1)
    begin = start.astype(jnp.float32).reshape(rows_n, width)
    context = layer_norm(flipped.astype(jnp.float32), gain_context).reshape(rows_n, width)
    normed = layer_norm(begin, gain_self)
    qkv = jnp.einsum("rd,kdc->krc", normed, self_qkv, preferred_element_type=jnp.float32).astype(
        jnp.bfloat16
    )
    term = jnp.dot(
        attend(qkv[0], qkv[1], qkv[2], views_n), self_out, preferred_element_type=jnp.float32
    )
    resid = begin + mp_allreduce(term.astype(jnp.bfloat16))
    normed = layer_norm(resid, gain_query)
    query = jnp.dot(normed, cross_query, preferred_element_type=jnp.float32).astype(jnp.bfloat16)
    keyval = jnp.einsum(
        "rd,kdc->krc", context, cross_kv, preferred_element_type=jnp.float32
    ).astype(jnp.bfloat16)
    term = jnp.dot(
        attend(query, keyval[0], keyval[1], views_n), cross_out, preferred_element_type=jnp.float32
    )
    resid = resid + mp_allreduce(term.astype(jnp.bfloat16))
    normed = layer_norm(resid, gain_mlp)
    hidden = jax.nn.gelu(
        jnp.dot(normed, mlp_up, preferred_element_type=jnp.float32), approximate=False
    )
    term = jnp.dot(hidden.astype(jnp.bfloat16), mlp_down, preferred_element_type=jnp.float32)
    offset = lax.axis_index("mp") * quarter
    final = lax.dynamic_slice_in_dim(resid, offset, quarter, 1) + mp_reduce_cols(
        term.astype(jnp.bfloat16)
    )
    conf = confidence.reshape(views_n, TOKS)
    weighted = (final.reshape(views_n, TOKS, quarter) * conf[:, :, None]).reshape(
        views_n, TOKS * quarter
    )
    source = ids // img_dev
    slot = (ids % img_dev + 1).astype(jnp.float32)
    route = (source[None, :] == jnp.arange(owners_n)[:, None]).astype(jnp.float32)
    back = jnp.dot(route, weighted, precision=lax.Precision.HIGHEST)
    back_weight = jnp.dot(route, conf, precision=lax.Precision.HIGHEST)
    back_slot = jnp.dot(route, slot[:, None], precision=lax.Precision.HIGHEST)
    pad = jnp.zeros((owners_n, 128 - TOKS - 1), jnp.float32)
    payload = jnp.concatenate([back, back_weight, back_slot, pad], axis=1).astype(jnp.bfloat16)
    got = lax.all_to_all(payload, "pairs", split_axis=0, concat_axis=0, tiled=True).astype(
        jnp.float32
    )
    feat = got[:, : TOKS * quarter].reshape(owners_n, TOKS, quarter)
    got_weight = got[:, TOKS * quarter : TOKS * quarter + TOKS]
    got_slot = got[:, TOKS * quarter + TOKS]
    owner_match = (
        got_slot[None, :] == (jnp.arange(img_dev) + 1)[:, None].astype(jnp.float32)
    ).astype(jnp.float32)
    numer = jnp.einsum("ij,jtc->itc", owner_match, feat, precision=lax.Precision.HIGHEST)
    denom = jnp.dot(owner_match, got_weight, precision=lax.Precision.HIGHEST)
    result = numer / jnp.maximum(denom, 1.0)[:, :, None]
    return result.astype(jnp.bfloat16).reshape(img_dev * TOKS, quarter)


def solution(mesh):
    return jax.shard_map(
        per_device,
        mesh=mesh,
        in_specs=(
            P(("groups", "pairs"), "mp"),
            P(("groups", "pairs"), None),
            P(("groups", "pairs"), None),
            P(),
            P(),
            P(),
            P(),
            P(None, None, "mp"),
            P("mp", None),
            P(None, "mp"),
            P(None, None, "mp"),
            P("mp", None),
            P(None, "mp"),
            P("mp", None),
        ),
        out_specs=P(("groups", "pairs"), "mp"),
        check_vma=False,
    )
```

profile of v0, /device:TPU:0, one launch (start us, length us, event | category | flops | bytes accessed | tf_op | source)
XLA Modules:
  0.0 69.1 jit_solution(16886699572011220582)
XLA Ops:
  0.0 0.9 %reshape.280 = s32[4,1]{0,1:T(1,128)S(1)} reshape(s32[2,2]{1,0:T(2,128)} %param.15) | data formatting | bytes 32 | tf_op jit(solution)/shard_map/reshape | solution.py:118
  0.9 0.8 %reshape.278 = s32[4]{0:T(128)S(1)} reshape(s32[2,2]{1,0:T(2,128)} %param.15) | data formatting | bytes 32 | tf_op jit(solution)/shard_map/reshape | solution.py:118
  1.6 15.3 %all_gather.3 = bf16[256,192]{1,0:T(8,128)(2,1)S(1)} all-gather(bf16[64,192]{1,0:T(8,128)(2,1)} %param.14), channel_id=1, replica_groups=mesh['groups'=2,'pairs'=4,'mp'=4] {'pairs'}, dimensions={0}, use_global_device_ids=true | all-gather | bytes 122880 | tf_op jit(solution)/shard_map/all_gather | solution.py:115
  16.9 0.6 gather_fusion
  17.6 0.7 compare_and_fusion
  18.9 1.6 %collective-permute-start.1 = (bf16[4,32,384]{2,1,0:T(8,128)(2,1)S(1)}, bf16[4,32,384]{2,1,0:T(8,128)(2,1)S(1)}, u32[]{:S(2)}, u32[]{:S(2)}) collective-permute-start(bf16[4,32,384]{2,1,0:T(8,128)(2,1)S(1)} %maximum_select_fusion.3), channel_id=1, source_target_pairs={{0,2},{1,3},{2,0},{3,1},{4,6},{5,7},{6,4},{7,5},{8,10},{9,11},{10,... | collective-permute-start | bytes 294920 | tf_op jit(solution)/shard_map/ppermute | solution.py:32
  20.7 3.2 %collective-permute-done.1 = bf16[4,32,384]{2,1,0:T(8,128)(2,1)S(1)} collective-permute-done((bf16[4,32,384]{2,1,0:T(8,128)(2,1)S(1)}, bf16[4,32,384]{2,1,0:T(8,128)(2,1)S(1)}, u32[]{:S(2)}, u32[]{:S(2)}) %collective-permute-start.1) | collective-permute-done | bytes 98336 | tf_op jit(solution)/shard_map/ppermute | solution.py:32
  24.9 0.5 fusion.33
  26.2 0.3 fusion.7
  27.3 0.3 copy-done.1
  27.6 0.3 fusion.149
  27.9 0.5 collective-permute-done.2
  28.5 1.6 %collective-permute-start.3 = (bf16[64,768]{1,0:T(8,128)(2,1)S(1)}, bf16[64,768]{1,0:T(8,128)(2,1)S(1)}, u32[]{:S(2)}, u32[]{:S(2)}) collective-permute-start(bf16[64,768]{1,0:T(8,128)(2,1)S(1)} %add_convert_fusion.1), channel_id=1, source_target_pairs={{0,2},{1,3},{2,0},{3,1},{4,6},{5,7},{6,4},{7,5},{8,10},{9,11},{10,... | collective-permute-start | bytes 294920 | tf_op jit(solution)/shard_map/ppermute | solution.py:32
  30.1 3.3 %collective-permute-done.3 = bf16[64,768]{1,0:T(8,128)(2,1)S(1)} collective-permute-done((bf16[64,768]{1,0:T(8,128)(2,1)S(1)}, bf16[64,768]{1,0:T(8,128)(2,1)S(1)}, u32[]{:S(2)}, u32[]{:S(2)}) %collective-permute-start.3) | collective-permute-done | bytes 98336 | tf_op jit(solution)/shard_map/ppermute | solution.py:32
  33.8 1.1 %collective-permute-done.4 = f32[64,768]{1,0:T(8,128)S(1)} collective-permute-done((f32[64,768]{1,0:T(8,128)S(1)}, f32[64,768]{1,0:T(8,128)S(1)}, u32[]{:S(2)}, u32[]{:S(2)}) %collective-permute-start.4) | collective-permute-done | bytes 196640 | tf_op jit(solution)/shard_map/ppermute | solution.py:32
  35.4 0.3 convolution_convert_fusion.6
  35.8 0.2 convolution_multiply_fusion
  36.2 0.3 fusion.8
  37.2 1.2 %collective-permute-done.5 = bf16[64,768]{1,0:T(8,128)(2,1)S(1)} collective-permute-done((bf16[64,768]{1,0:T(8,128)(2,1)S(1)}, bf16[64,768]{1,0:T(8,128)(2,1)S(1)}, u32[]{:S(2)}, u32[]{:S(2)}) %collective-permute-start.5) | collective-permute-done | bytes 98336 | tf_op jit(solution)/shard_map/ppermute | solution.py:32
  38.4 1.6 %collective-permute-start.6 = (bf16[64,768]{1,0:T(8,128)(2,1)S(1)}, bf16[64,768]{1,0:T(8,128)(2,1)S(1)}, u32[]{:S(2)}, u32[]{:S(2)}) collective-permute-start(bf16[64,768]{1,0:T(8,128)(2,1)S(1)} %add_convert_fusion), channel_id=1, source_target_pairs={{0,2},{1,3},{2,0},{3,1},{4,6},{5,7},{6,4},{7,5},{8,10},{9,11},{10,... | collective-permute-start | bytes 294920 | tf_op jit(solution)/shard_map/ppermute | solution.py:32
  40.3 3.1 %collective-permute-done.6 = bf16[64,768]{1,0:T(8,128)(2,1)S(1)} collective-permute-done((bf16[64,768]{1,0:T(8,128)(2,1)S(1)}, bf16[64,768]{1,0:T(8,128)(2,1)S(1)}, u32[]{:S(2)}, u32[]{:S(2)}) %collective-permute-start.6) | collective-permute-done | bytes 98336 | tf_op jit(solution)/shard_map/ppermute | solution.py:32
  43.5 1.4 %collective-permute-done.7 = f32[64,768]{1,0:T(8,128)S(1)} collective-permute-done((f32[64,768]{1,0:T(8,128)S(1)}, f32[64,768]{1,0:T(8,128)S(1)}, u32[]{:S(2)}, u32[]{:S(2)}) %collective-permute-start.7) | collective-permute-done | bytes 196640 | tf_op jit(solution)/shard_map/ppermute | solution.py:32
  45.3 1.5 %convolution_convert_fusion.1 = bf16[128,768]{1,0:T(8,128)(2,1)S(1)} fusion(bf16[768,768]{1,0:T(8,128)(2,1)S(1)} %copy-done, bf16[768,768]{1,0:T(8,128)(2,1)S(1)} %copy-done.6, f32[128,768]{1,0:T(8,128)S(1)} %get-tuple-element.6, f32[768]{0:T(1024)S(1)} %copy-done.11, f32[128]{0:T(128)S(1)} %add_rsqrt_fusion.1, f32[128]{0:T(128)S(1)} %broadcast_multiply_fusion.1), kind=kOutput, calls=%fused_computation.7 | convolution fusion | flops 308871168 | bytes 2953216 | tf_op jit(solution)/shard_map/dot_general | solution.py:148
  47.7 1.0 %collective-permute-done.8 = bf16[128,2,192]{2,0,1:T(8,128)(2,1)S(1)} collective-permute-done((bf16[128,2,192]{2,0,1:T(8,128)(2,1)S(1)}, bf16[128,2,192]{2,0,1:T(8,128)(2,1)S(1)}, u32[]{:S(2)}, u32[]{:S(2)}) %collective-permute-start.8) | collective-permute-done | bytes 98336 | tf_op jit(solution)/shard_map/ppermute | solution.py:32
  48.7 1.6 %collective-permute-start.9 = (f32[128,192]{1,0:T(8,128)S(1)}, f32[128,192]{1,0:T(8,128)S(1)}, u32[]{:S(2)}, u32[]{:S(2)}) collective-permute-start(f32[128,192]{1,0:T(8,128)S(1)} %select_bitcast_fusion), channel_id=1, source_target_pairs={{0,2},{1,3},{2,0},{3,1},{4,6},{5,7},{6,4},{7,5},{8,10},{9,11},{10,... | collective-permute-start | bytes 294920 | tf_op jit(solution)/shard_map/ppermute | solution.py:32
  50.4 3.9 %collective-permute-done.9 = f32[128,192]{1,0:T(8,128)S(1)} collective-permute-done((f32[128,192]{1,0:T(8,128)S(1)}, f32[128,192]{1,0:T(8,128)S(1)}, u32[]{:S(2)}, u32[]{:S(2)}) %collective-permute-start.9) | collective-permute-done | bytes 98336 | tf_op jit(solution)/shard_map/ppermute | solution.py:32
  54.9 0.5 broadcast.282
  55.4 0.7 reduce.2
  56.1 0.7 %reshape.313 = bf16[4,2,3136]{2,1,0:T(2,128)(2,1)} reshape(bf16[4,6272]{1,0:T(4,128)(2,1)S(1)} %reduce.2) | data formatting | bytes 100352
  56.8 5.0 %all-to-all-start = ((bf16[4,2,3136]{2,1,0:T(2,128)(2,1)}), bf16[4,2,3136]{2,1,0:T(2,128)(2,1)S(1)}, u32[]{:S(2)}, u32[]{:S(2)}) async-start(bf16[4,2,3136]{2,1,0:T(2,128)(2,1)} %reshape.313), calls=%async_computation | async-start | bytes 102400 | tf_op jit(solution)/shard_map/all_to_all | solution.py:165
  61.8 5.7 %all-to-all-done = bf16[4,2,3136]{2,1,0:T(2,128)(2,1)S(1)} async-done(((bf16[4,2,3136]{2,1,0:T(2,128)(2,1)}), bf16[4,2,3136]{2,1,0:T(2,128)(2,1)S(1)}, u32[]{:S(2)}, u32[]{:S(2)}) %all-to-all-start) | async-done | bytes 50208 | tf_op jit(solution)/shard_map/all_to_all | solution.py:165
  68.5 0.6 copy.95
  (118 shorter events, 8.6 us)
Async XLA Ops:
  0.0 45.3 %copy-start = (bf16[768,768]{1,0:T(8,128)(2,1)S(1)}, bf16[768,768]{1,0:T(8,128)(2,1)}, u32[]{:S(2)}) copy-start(bf16[768,768]{1,0:T(8,128)(2,1)} %param.27) | copy-start | bytes 3538948
  17.5 1.3 %collective-permute-start = (bf16[4,32,192]{2,1,0:T(8,128)(2,1)S(1)}, bf16[4,32,192]{2,1,0:T(8,128)(2,1)S(1)}, u32[]{:S(2)}, u32[]{:S(2)}) collective-permute-start(bf16[4,32,192]{2,1,0:T(8,128)(2,1)S(1)} %broadcast_select_fusion.6), channel_id=1, source_target_pairs={{0,1},{1,0},{2,3},{3,2},{4,5},{5,4},{6,7},{7,6},{8,9},{9,8},{10,11... | collective-permute-start | bytes 147464 | tf_op jit(solution)/shard_map/ppermute | solution.py:32
  18.9 5.1 %collective-permute-start.1 = (bf16[4,32,384]{2,1,0:T(8,128)(2,1)S(1)}, bf16[4,32,384]{2,1,0:T(8,128)(2,1)S(1)}, u32[]{:S(2)}, u32[]{:S(2)}) collective-permute-start(bf16[4,32,384]{2,1,0:T(8,128)(2,1)S(1)} %maximum_select_fusion.3), channel_id=1, source_target_pairs={{0,2},{1,3},{2,0},{3,1},{4,6},{5,7},{6,4},{7,5},{8,10},{9,11},{10,... | collective-permute-start | bytes 294920 | tf_op jit(solution)/shard_map/ppermute | solution.py:32
  20.6 4.3 %copy-start.7 = (bf16[3,768,192]{1,2,0:T(8,128)(2,1)S(1)}, bf16[3,768,192]{1,2,0:T(8,128)(2,1)}, u32[]{:S(2)}) copy-start(bf16[3,768,192]{1,2,0:T(8,128)(2,1)} %param.21) | copy-start | bytes 2654212
  20.6 4.3 %copy-start.9 = (f32[768]{0:T(1024)S(1)}, f32[768]{0:T(1024)}, u32[]{:S(2)}) copy-start(f32[768]{0:T(1024)} %param.17) | copy-start | bytes 9220
  25.9 1.0 %copy-start.2 = (bf16[192,768]{1,0:T(8,128)(2,1)S(1)}, bf16[192,768]{1,0:T(8,128)(2,1)}, u32[]{:S(2)}) copy-start(bf16[192,768]{1,0:T(8,128)(2,1)} %param.22) | copy-start | bytes 884740
  26.2 1.0 %copy-start.4 = (f32[768]{0:T(1024)S(1)}, f32[768]{0:T(1024)}, u32[]{:S(2)}) copy-start(f32[768]{0:T(1024)} %param.19) | copy-start | bytes 9220
  26.5 1.1 %copy-start.1 = (bf16[2,768,192]{1,2,0:T(8,128)(2,1)S(1)}, bf16[2,768,192]{1,2,0:T(8,128)(2,1)}, u32[]{:S(2)}) copy-start(bf16[2,768,192]{1,2,0:T(8,128)(2,1)} %param.24) | copy-start | bytes 1769476
  27.1 1.4 %collective-permute-start.2 = (bf16[64,768]{1,0:T(8,128)(2,1)S(1)}, bf16[64,768]{1,0:T(8,128)(2,1)S(1)}, u32[]{:S(2)}, u32[]{:S(2)}) collective-permute-start(bf16[64,768]{1,0:T(8,128)(2,1)S(1)} %broadcast_select_fusion.5), channel_id=1, source_target_pairs={{0,1},{1,0},{2,3},{3,2},{4,5},{5,4},{6,7},{7,6},{8,9},{9,8},{10,11... | collective-permute-start | bytes 294920 | tf_op jit(solution)/shard_map/ppermute | solution.py:32
  28.5 4.9 %collective-permute-start.3 = (bf16[64,768]{1,0:T(8,128)(2,1)S(1)}, bf16[64,768]{1,0:T(8,128)(2,1)S(1)}, u32[]{:S(2)}, u32[]{:S(2)}) collective-permute-start(bf16[64,768]{1,0:T(8,128)(2,1)S(1)} %add_convert_fusion.1), channel_id=1, source_target_pairs={{0,2},{1,3},{2,0},{3,1},{4,6},{5,7},{6,4},{7,5},{8,10},{9,11},{10,... | collective-permute-start | bytes 294920 | tf_op jit(solution)/shard_map/ppermute | solution.py:32
  33.4 1.5 %collective-permute-start.4 = (f32[64,768]{1,0:T(8,128)S(1)}, f32[64,768]{1,0:T(8,128)S(1)}, u32[]{:S(2)}, u32[]{:S(2)}) collective-permute-start(f32[64,768]{1,0:T(8,128)S(1)} %convert_add_fusion.3), channel_id=1, source_target_pairs={{0,1},{1,0},{2,3},{3,2},{4,5},{5,4},{6,7},{7,6},{8,9},{9,8},{10,11... | collective-permute-start | bytes 589832 | tf_op jit(solution)/shard_map/ppermute | solution.py:32
  33.5 1.8 %copy-start.8 = (bf16[768,192]{0,1:T(8,128)(2,1)S(1)}, bf16[768,192]{0,1:T(8,128)(2,1)}, u32[]{:S(2)}) copy-start(bf16[768,192]{0,1:T(8,128)(2,1)} %param.23) | copy-start | bytes 884740
  33.5 1.8 %copy-start.10 = (f32[768]{0:T(1024)S(1)}, f32[768]{0:T(1024)}, u32[]{:S(2)}) copy-start(f32[768]{0:T(1024)} %param.18) | copy-start | bytes 9220
  35.8 1.0 %copy-start.3 = (bf16[192,768]{1,0:T(8,128)(2,1)S(1)}, bf16[192,768]{1,0:T(8,128)(2,1)}, u32[]{:S(2)}) copy-start(bf16[192,768]{1,0:T(8,128)(2,1)} %param.25) | copy-start | bytes 884740
  36.1 3.8 %copy-start.5 = (f32[2,64]{1,0:T(2,128)S(1)}, f32[2,64]{1,0:T(2,128)}, u32[]{:S(2)}) copy-start(f32[2,64]{1,0:T(2,128)} %param.16) | copy-start | bytes 1540
  37.0 1.4 %collective-permute-start.5 = (bf16[64,768]{1,0:T(8,128)(2,1)S(1)}, bf16[64,768]{1,0:T(8,128)(2,1)S(1)}, u32[]{:S(2)}, u32[]{:S(2)}) collective-permute-start(bf16[64,768]{1,0:T(8,128)(2,1)S(1)} %broadcast_select_fusion.2), channel_id=1, source_target_pairs={{0,1},{1,0},{2,3},{3,2},{4,5},{5,4},{6,7},{7,6},{8,9},{9,8},{10,11... | collective-permute-start | bytes 294920 | tf_op jit(solution)/shard_map/ppermute | solution.py:32
  38.4 4.9 %collective-permute-start.6 = (bf16[64,768]{1,0:T(8,128)(2,1)S(1)}, bf16[64,768]{1,0:T(8,128)(2,1)S(1)}, u32[]{:S(2)}, u32[]{:S(2)}) collective-permute-start(bf16[64,768]{1,0:T(8,128)(2,1)S(1)} %add_convert_fusion), channel_id=1, source_target_pairs={{0,2},{1,3},{2,0},{3,1},{4,6},{5,7},{6,4},{7,5},{8,10},{9,11},{10,... | collective-permute-start | bytes 294920 | tf_op jit(solution)/shard_map/ppermute | solution.py:32
  43.4 1.5 %collective-permute-start.7 = (f32[64,768]{1,0:T(8,128)S(1)}, f32[64,768]{1,0:T(8,128)S(1)}, u32[]{:S(2)}, u32[]{:S(2)}) collective-permute-start(f32[64,768]{1,0:T(8,128)S(1)} %convert_add_fusion.2), channel_id=1, source_target_pairs={{0,1},{1,0},{2,3},{3,2},{4,5},{5,4},{6,7},{7,6},{8,9},{9,8},{10,11... | collective-permute-start | bytes 589832 | tf_op jit(solution)/shard_map/ppermute | solution.py:32
  43.5 1.8 %copy-start.6 = (bf16[768,768]{1,0:T(8,128)(2,1)S(1)}, bf16[768,768]{1,0:T(8,128)(2,1)}, u32[]{:S(2)}) copy-start(bf16[768,768]{1,0:T(8,128)(2,1)} %param.26) | copy-start | bytes 3538948
  43.5 1.8 %copy-start.11 = (f32[768]{0:T(1024)S(1)}, f32[768]{0:T(1024)}, u32[]{:S(2)}) copy-start(f32[768]{0:T(1024)} %param.20) | copy-start | bytes 9220
  47.2 1.4 %collective-permute-start.8 = (bf16[128,2,192]{2,0,1:T(8,128)(2,1)S(1)}, bf16[128,2,192]{2,0,1:T(8,128)(2,1)S(1)}, u32[]{:S(2)}, u32[]{:S(2)}) collective-permute-start(bf16[128,2,192]{2,0,1:T(8,128)(2,1)S(1)} %select_bitcast_fusion.1), channel_id=1, source_target_pairs={{0,1},{1,0},{2,3},{3,2},{4,5},{5,4},{6,7},{7,6},{8,9},{9,8},{10,11... | collective-permute-start | bytes 294920 | tf_op jit(solution)/shard_map/ppermute | solution.py:32
  48.7 5.6 %collective-permute-start.9 = (f32[128,192]{1,0:T(8,128)S(1)}, f32[128,192]{1,0:T(8,128)S(1)}, u32[]{:S(2)}, u32[]{:S(2)}) collective-permute-start(f32[128,192]{1,0:T(8,128)S(1)} %select_bitcast_fusion), channel_id=1, source_target_pairs={{0,2},{1,3},{2,0},{3,1},{4,6},{5,7},{6,4},{7,5},{8,10},{9,11},{10,... | collective-permute-start | bytes 294920 | tf_op jit(solution)/shard_map/ppermute | solution.py:32
  56.8 10.7 %all-to-all-start = ((bf16[4,2,3136]{2,1,0:T(2,128)(2,1)}), bf16[4,2,3136]{2,1,0:T(2,128)(2,1)S(1)}, u32[]{:S(2)}, u32[]{:S(2)}) async-start(bf16[4,2,3136]{2,1,0:T(2,128)(2,1)} %reshape.313), calls=%async_computation | async-start | bytes 102400 | tf_op jit(solution)/shard_map/all_to_all | solution.py:165
where the time goes:
time: 69.4 us; the launch traced here: 69.1 us
  waiting for transfers between devices  24.7 us (36%)
  blocking collectives  15.3 us (22%)
  starting transfers between devices  11.8 us (17%)
  local copies, waits for them, and re-layouts  7.6 us (11%)
  matrix products  4.83 us (7%)
  other arithmetic  4.32 us (6%)
    ppermute x10, waiting for transfers between devices, swap(): return lax.ppermute(values, 'mp', pairs)  19 us
    all_gather x1, blocking collectives, per_device(): lax.all_gather(tokens, 'pairs', axis=0, tiled=True)  15.3 us
    ppermute x10, starting transfers between devices, swap(): return lax.ppermute(values, 'mp', pairs)  6.86 us
    all_to_all x1, waiting for transfers between devices, per_device(): lax.all_to_all(payload, 'pairs', split_axis=0, concat_axis=0, tiled=True)  5.7 us
    all_to_all x1, starting transfers between devices, per_device(): lax.all_to_all(payload, 'pairs', split_axis=0, concat_axis=0, tiled=True)  4.97 us
    unnamed x29, local copies, waits for them, and re-layouts  1.71 us
    reshape x2, local copies, waits for them, and re-layouts, per_device(): ids = pair_list.reshape(views_n)  1.61 us
    dot_general x1, matrix products, per_device(): jnp.dot(hidden.astype(jnp.bfloat16), mlp_down, preferred_element_type=jnp...  1.45 us
  transfers between devices with their start and end apart: 11, of which 11 were waited for; matrix products, arithmetic and copies ran while one was open for 4% of the time, Pallas kernels for 0%

commit v1 on v0

--- a/solution.py
+++ b/solution.py
@@ -6,6 +6,26 @@
 HEAD = 64
 TOKS = 32
 EPSILON = 1e-06
+
+
+def _divide_tails(own_rows, array_dim, array_here):
+    reached = own_rows.shape
+    return jnp.moveaxis(
+        own_rows.reshape(
+            *reached[:array_dim],
+            array_here,
+            reached[array_dim] // array_here,
+            *reached[array_dim + 1 :]
+        ),
+        array_dim,
+        0,
+    )
+
+
+def post_samples_over_axis(slab_in, row_dim):
+    prior = list(slab_in.shape[1:])
+    prior[row_dim] *= slab_in.shape[0]
+    return jnp.moveaxis(slab_in, 0, row_dim).reshape(prior)
 
 
 def layer_norm(values, gain):
@@ -162,9 +182,22 @@
     back_slot = jnp.dot(route, slot[:, None], precision=lax.Precision.HIGHEST)
     pad = jnp.zeros((owners_n, 128 - TOKS - 1), jnp.float32)
     payload = jnp.concatenate([back, back_weight, back_slot, pad], axis=1).astype(jnp.bfloat16)
-    got = lax.all_to_all(payload, "pairs", split_axis=0, concat_axis=0, tiled=True).astype(
-        jnp.float32
-    )
+
+    def process_target(xs, work_x, dev_axis, state):
+        v_now, outer = (lax.axis_size(dev_axis), lax.axis_index(dev_axis))
+        z = _divide_tails(xs, work_x, v_now)
+        views = [z[outer]]
+        for idx in range(1, v_now):
+            y = z[outer ^ idx]
+            views.append(
+                lax.ppermute(
+                    y, axis_name=dev_axis, perm=[(hop_no, hop_no ^ idx) for hop_no in range(v_now)]
+                )
+            )
+        z = jnp.stack(views, axis=0)[outer ^ jnp.arange(v_now)]
+        return post_samples_over_axis(z, state)
+
+    got = process_target(payload, 0, "pairs", 0).astype(jnp.float32)
     feat = got[:, : TOKS * quarter].reshape(owners_n, TOKS, quarter)
     got_weight = got[:, TOKS * quarter : TOKS * quarter + TOKS]
     got_slot = got[:, TOKS * quarter + TOKS]

time: 69.4 us -> 65.9 us (0.950)
  waiting for transfers between devices: 24.7 us -> 23 us
    all_to_all x1 -> x0, waiting for transfers between devices: 5.7 us -> none  [per_device(): lax.all_to_all(payload, 'pairs', split_axis=0, concat_axis=0, tiled=True)]
    all_to_all x1 -> x0, starting transfers between devices: 4.97 us -> none  [per_device(): lax.all_to_all(payload, 'pairs', split_axis=0, concat_axis=0, tiled=True)]
    ppermute x0 -> x3, starting transfers between devices: none -> 4.45 us  [process_target(): lax.ppermute(y, axis_name=dev_axis, perm=[(hop_no, hop_no ^ idx) for hop_...]
    ppermute x0 -> x3, waiting for transfers between devices: none -> 4.04 us  [process_target(): lax.ppermute(y, axis_name=dev_axis, perm=[(hop_no, hop_no ^ idx) for hop_...]
    unnamed x29 -> x26, local copies, waits for them, and re-layouts: 1.71 us -> 0.82 us
  transfers between devices with their start and end apart: 11 -> 13, of which waited for: 11 -> 12; matrix products, arithmetic and copies ran while one was open for 4% -> 4% of each run, Pallas kernels for 0% -> 0%
where the time goes in v1:
time: 65.9 us; the launch traced here: 65.7 us
  waiting for transfers between devices  23 us (35%)
  blocking collectives  15.3 us (23%)
  starting transfers between devices  11.3 us (17%)
  local copies, waits for them, and re-layouts  6.91 us (10%)
  matrix products  4.83 us (7%)
  other arithmetic  3.8 us (6%)
    ppermute x10, waiting for transfers between devices, swap(): return lax.ppermute(values, 'mp', pairs)  19 us
    all_gather x1, blocking collectives, per_device(): lax.all_gather(tokens, 'pairs', axis=0, tiled=True)  15.3 us
    ppermute x10, starting transfers between devices, swap(): return lax.ppermute(values, 'mp', pairs)  6.86 us
    ppermute x3, starting transfers between devices, process_target(): lax.ppermute(y, axis_name=dev_axis, perm=[(hop_no, hop_no ^ idx) for hop_...  4.45 us
    ppermute x3, waiting for transfers between devices, process_target(): lax.ppermute(y, axis_name=dev_axis, perm=[(hop_no, hop_no ^ idx) for hop_...  4.04 us
    reshape x2, local copies, waits for them, and re-layouts, per_device(): ids = pair_list.reshape(views_n)  1.61 us
    dot_general x1, matrix products, per_device(): jnp.dot(hidden.astype(jnp.bfloat16), mlp_down, preferred_element_type=jnp...  1.45 us
  transfers between devices with their start and end apart: 13, of which 12 were waited for; matrix products, arithmetic and copies ran while one was open for 4% of the time, Pallas kernels for 0%

profile of v1, /device:TPU:0, one launch (start us, length us, event | category | flops | bytes accessed | tf_op | source)
XLA Modules:
  0.0 65.7 jit_solution(18272050686934378141)
XLA Ops:
  0.0 0.9 %reshape.253 = s32[4,1]{0,1:T(1,128)S(1)} reshape(s32[2,2]{1,0:T(2,128)} %param.15) | data formatting | bytes 32 | tf_op jit(solution)/shard_map/reshape | solution.py:138
  0.9 0.8 %reshape.251 = s32[4]{0:T(128)S(1)} reshape(s32[2,2]{1,0:T(2,128)} %param.15) | data formatting | bytes 32 | tf_op jit(solution)/shard_map/reshape | solution.py:138
  1.6 15.3 %all_gather.3 = bf16[256,192]{1,0:T(8,128)(2,1)S(1)} all-gather(bf16[64,192]{1,0:T(8,128)(2,1)} %param.14), channel_id=1, replica_groups=mesh['groups'=2,'pairs'=4,'mp'=4] {'pairs'}, dimensions={0}, use_global_device_ids=true | all-gather | bytes 122880 | tf_op jit(solution)/shard_map/all_gather | solution.py:135
  16.9 0.6 gather_fusion
  17.6 0.7 %compare_and_fusion = pred[2,2]{1,0:T(4,128)(4,1)S(1)} fusion(s32[2,2]{1,0:T(2,128)} %param.15), kind=kLoop, calls=%fused_computation.156 | loop fusion | flops 24 | bytes 20 | tf_op jit(solution)/shard_map/jit(_take)/and | solution.py:139
  18.9 1.6 %collective-permute-start.1 = (bf16[4,32,384]{2,1,0:T(8,128)(2,1)S(1)}, bf16[4,32,384]{2,1,0:T(8,128)(2,1)S(1)}, u32[]{:S(2)}, u32[]{:S(2)}) collective-permute-start(bf16[4,32,384]{2,1,0:T(8,128)(2,1)S(1)} %maximum_select_fusion.3), channel_id=1, source_target_pairs={{0,2},{1,3},{2,0},{3,1},{4,6},{5,7},{6,4},{7,5},{8,10},{9,11},{10,... | collective-permute-start | bytes 294920 | tf_op jit(solution)/shard_map/ppermute | solution.py:52
  20.7 3.2 %collective-permute-done.1 = bf16[4,32,384]{2,1,0:T(8,128)(2,1)S(1)} collective-permute-done((bf16[4,32,384]{2,1,0:T(8,128)(2,1)S(1)}, bf16[4,32,384]{2,1,0:T(8,128)(2,1)S(1)}, u32[]{:S(2)}, u32[]{:S(2)}) %collective-permute-start.1) | collective-permute-done | bytes 98336 | tf_op jit(solution)/shard_map/ppermute | solution.py:52
  24.9 0.5 fusion.31
  25.9 0.2 convolution_multiply_fusion.1
  26.2 0.3 fusion.6
  27.3 0.3 copy-done.1
  27.6 0.3 fusion.148
  27.9 0.5 collective-permute-done.2
  28.5 1.6 %collective-permute-start.3 = (bf16[64,768]{1,0:T(8,128)(2,1)S(1)}, bf16[64,768]{1,0:T(8,128)(2,1)S(1)}, u32[]{:S(2)}, u32[]{:S(2)}) collective-permute-start(bf16[64,768]{1,0:T(8,128)(2,1)S(1)} %add_convert_fusion.1), channel_id=1, source_target_pairs={{0,2},{1,3},{2,0},{3,1},{4,6},{5,7},{6,4},{7,5},{8,10},{9,11},{10,... | collective-permute-start | bytes 294920 | tf_op jit(solution)/shard_map/ppermute | solution.py:52
  30.1 3.3 %collective-permute-done.3 = bf16[64,768]{1,0:T(8,128)(2,1)S(1)} collective-permute-done((bf16[64,768]{1,0:T(8,128)(2,1)S(1)}, bf16[64,768]{1,0:T(8,128)(2,1)S(1)}, u32[]{:S(2)}, u32[]{:S(2)}) %collective-permute-start.3) | collective-permute-done | bytes 98336 | tf_op jit(solution)/shard_map/ppermute | solution.py:52
  33.8 1.1 %collective-permute-done.4 = f32[64,768]{1,0:T(8,128)S(1)} collective-permute-done((f32[64,768]{1,0:T(8,128)S(1)}, f32[64,768]{1,0:T(8,128)S(1)}, u32[]{:S(2)}, u32[]{:S(2)}) %collective-permute-start.4) | collective-permute-done | bytes 196640 | tf_op jit(solution)/shard_map/ppermute | solution.py:52
  35.4 0.3 convolution_convert_fusion.6
  36.2 0.3 fusion.7
  37.5 0.9 %collective-permute-done.5 = bf16[64,768]{1,0:T(8,128)(2,1)S(1)} collective-permute-done((bf16[64,768]{1,0:T(8,128)(2,1)S(1)}, bf16[64,768]{1,0:T(8,128)(2,1)S(1)}, u32[]{:S(2)}, u32[]{:S(2)}) %collective-permute-start.5) | collective-permute-done | bytes 98336 | tf_op jit(solution)/shard_map/ppermute | solution.py:52
  38.4 1.6 %collective-permute-start.6 = (bf16[64,768]{1,0:T(8,128)(2,1)S(1)}, bf16[64,768]{1,0:T(8,128)(2,1)S(1)}, u32[]{:S(2)}, u32[]{:S(2)}) collective-permute-start(bf16[64,768]{1,0:T(8,128)(2,1)S(1)} %add_convert_fusion), channel_id=1, source_target_pairs={{0,2},{1,3},{2,0},{3,1},{4,6},{5,7},{6,4},{7,5},{8,10},{9,11},{10,... | collective-permute-start | bytes 294920 | tf_op jit(solution)/shard_map/ppermute | solution.py:52
  40.2 3.1 %collective-permute-done.6 = bf16[64,768]{1,0:T(8,128)(2,1)S(1)} collective-permute-done((bf16[64,768]{1,0:T(8,128)(2,1)S(1)}, bf16[64,768]{1,0:T(8,128)(2,1)S(1)}, u32[]{:S(2)}, u32[]{:S(2)}) %collective-permute-start.6) | collective-permute-done | bytes 98336 | tf_op jit(solution)/shard_map/ppermute | solution.py:52
  43.6 1.3 %collective-permute-done.7 = f32[64,768]{1,0:T(8,128)S(1)} collective-permute-done((f32[64,768]{1,0:T(8,128)S(1)}, f32[64,768]{1,0:T(8,128)S(1)}, u32[]{:S(2)}, u32[]{:S(2)}) %collective-permute-start.7) | collective-permute-done | bytes 196640 | tf_op jit(solution)/shard_map/ppermute | solution.py:52
  45.3 1.4 %convolution_convert_fusion.1 = bf16[128,768]{1,0:T(8,128)(2,1)S(1)} fusion(bf16[768,768]{1,0:T(8,128)(2,1)S(1)} %copy-done, bf16[768,768]{1,0:T(8,128)(2,1)S(1)} %copy-done.6, f32[128,768]{1,0:T(8,128)S(1)} %get-tuple-element.6, f32[768]{0:T(1024)S(1)} %copy-done.11, f32[128]{0:T(128)S(1)} %add_rsqrt_fusion.1, f32[128]{0:T(128)S(1)} %broadcast_multiply_fusion.1), kind=kOutput, calls=%fused_computation.7 | convolution fusion | flops 308871168 | bytes 2953216 | tf_op jit(solution)/shard_map/dot_general | solution.py:168
  47.4 1.2 %collective-permute-done.8 = bf16[128,2,192]{2,0,1:T(8,128)(2,1)S(1)} collective-permute-done((bf16[128,2,192]{2,0,1:T(8,128)(2,1)S(1)}, bf16[128,2,192]{2,0,1:T(8,128)(2,1)S(1)}, u32[]{:S(2)}, u32[]{:S(2)}) %collective-permute-start.8) | collective-permute-done | bytes 98336 | tf_op jit(solution)/shard_map/ppermute | solution.py:52
  48.7 1.6 %collective-permute-start.9 = (f32[128,192]{1,0:T(8,128)S(1)}, f32[128,192]{1,0:T(8,128)S(1)}, u32[]{:S(2)}, u32[]{:S(2)}) collective-permute-start(f32[128,192]{1,0:T(8,128)S(1)} %select_bitcast_fusion), channel_id=1, source_target_pairs={{0,2},{1,3},{2,0},{3,1},{4,6},{5,7},{6,4},{7,5},{8,10},{9,11},{10,... | collective-permute-start | bytes 294920 | tf_op jit(solution)/shard_map/ppermute | solution.py:52
  50.3 4.1 %collective-permute-done.9 = f32[128,192]{1,0:T(8,128)S(1)} collective-permute-done((f32[128,192]{1,0:T(8,128)S(1)}, f32[128,192]{1,0:T(8,128)S(1)}, u32[]{:S(2)}, u32[]{:S(2)}) %collective-permute-start.9) | collective-permute-done | bytes 98336 | tf_op jit(solution)/shard_map/ppermute | solution.py:52
  55.0 3.8 %collective-permute-start.12 = (bf16[1,6272]{1,0:T(2,128)(2,1)S(1)}, bf16[1,6272]{1,0:T(2,128)(2,1)S(1)}, u32[]{:S(2)}, u32[]{:S(2)}) collective-permute-start(bf16[1,6272]{1,0:T(2,128)(2,1)S(1)} %get-tuple-element.21), channel_id=1, source_target_pairs={{0,12},{4,8},{8,4},{12,0},{1,13},{5,9},{9,5},{13,1},{2,14},{6,10},... | collective-permute-start | bytes 37640 | tf_op jit(solution)/shard_map/ppermute | solution.py:193
  58.8 0.7 %collective-permute-start.10 = (bf16[1,6272]{1,0:T(2,128)(2,1)S(1)}, bf16[1,6272]{1,0:T(2,128)(2,1)S(1)}, u32[]{:S(2)}, u32[]{:S(2)}) collective-permute-start(bf16[1,6272]{1,0:T(2,128)(2,1)S(1)} %get-tuple-element.23), channel_id=1, source_target_pairs={{0,4},{4,0},{8,12},{12,8},{1,5},{5,1},{9,13},{13,9},{2,6},{6,2},{1... | collective-permute-start | bytes 37640 | tf_op jit(solution)/shard_map/ppermute | solution.py:193
  59.5 1.3 %collective-permute-done.12 = bf16[1,6272]{1,0:T(2,128)(2,1)S(1)} collective-permute-done((bf16[1,6272]{1,0:T(2,128)(2,1)S(1)}, bf16[1,6272]{1,0:T(2,128)(2,1)S(1)}, u32[]{:S(2)}, u32[]{:S(2)}) %collective-permute-start.12) | collective-permute-done | bytes 12576 | tf_op jit(solution)/shard_map/ppermute | solution.py:193
  60.8 2.7 %collective-permute-done.11 = bf16[1,6272]{1,0:T(2,128)(2,1)S(1)} collective-permute-done((bf16[1,6272]{1,0:T(2,128)(2,1)S(1)}, bf16[1,6272]{1,0:T(2,128)(2,1)S(1)}, u32[]{:S(2)}, u32[]{:S(2)}) %collective-permute-start.11) | collective-permute-done | bytes 12576 | tf_op jit(solution)/shard_map/ppermute | solution.py:193
  63.7 0.6 gather_fusion.1
  65.1 0.6 copy.47
  (122 shorter events, 8.7 us)
Async XLA Ops:
  0.0 45.3 %copy-start = (bf16[768,768]{1,0:T(8,128)(2,1)S(1)}, bf16[768,768]{1,0:T(8,128)(2,1)}, u32[]{:S(2)}) copy-start(bf16[768,768]{1,0:T(8,128)(2,1)} %param.27) | copy-start | bytes 3538948
  17.5 1.3 %collective-permute-start = (bf16[4,32,192]{2,1,0:T(8,128)(2,1)S(1)}, bf16[4,32,192]{2,1,0:T(8,128)(2,1)S(1)}, u32[]{:S(2)}, u32[]{:S(2)}) collective-permute-start(bf16[4,32,192]{2,1,0:T(8,128)(2,1)S(1)} %broadcast_select_fusion.6), channel_id=1, source_target_pairs={{0,1},{1,0},{2,3},{3,2},{4,5},{5,4},{6,7},{7,6},{8,9},{9,8},{10,11... | collective-permute-start | bytes 147464 | tf_op jit(solution)/shard_map/ppermute | solution.py:52
  18.9 5.1 %collective-permute-start.1 = (bf16[4,32,384]{2,1,0:T(8,128)(2,1)S(1)}, bf16[4,32,384]{2,1,0:T(8,128)(2,1)S(1)}, u32[]{:S(2)}, u32[]{:S(2)}) collective-permute-start(bf16[4,32,384]{2,1,0:T(8,128)(2,1)S(1)} %maximum_select_fusion.3), channel_id=1, source_target_pairs={{0,2},{1,3},{2,0},{3,1},{4,6},{5,7},{6,4},{7,5},{8,10},{9,11},{10,... | collective-permute-start | bytes 294920 | tf_op jit(solution)/shard_map/ppermute | solution.py:52
  20.6 4.3 %copy-start.7 = (bf16[3,768,192]{1,2,0:T(8,128)(2,1)S(1)}, bf16[3,768,192]{1,2,0:T(8,128)(2,1)}, u32[]{:S(2)}) copy-start(bf16[3,768,192]{1,2,0:T(8,128)(2,1)} %param.21) | copy-start | bytes 2654212
  20.6 4.3 %copy-start.9 = (f32[768]{0:T(1024)S(1)}, f32[768]{0:T(1024)}, u32[]{:S(2)}) copy-start(f32[768]{0:T(1024)} %param.17) | copy-start | bytes 9220
  25.9 1.0 %copy-start.2 = (bf16[192,768]{1,0:T(8,128)(2,1)S(1)}, bf16[192,768]{1,0:T(8,128)(2,1)}, u32[]{:S(2)}) copy-start(bf16[192,768]{1,0:T(8,128)(2,1)} %param.22) | copy-start | bytes 884740
  26.2 1.0 %copy-start.4 = (f32[768]{0:T(1024)S(1)}, f32[768]{0:T(1024)}, u32[]{:S(2)}) copy-start(f32[768]{0:T(1024)} %param.19) | copy-start | bytes 9220
  26.5 1.1 %copy-start.1 = (bf16[2,768,192]{1,2,0:T(8,128)(2,1)S(1)}, bf16[2,768,192]{1,2,0:T(8,128)(2,1)}, u32[]{:S(2)}) copy-start(bf16[2,768,192]{1,2,0:T(8,128)(2,1)} %param.24) | copy-start | bytes 1769476
  27.1 1.4 %collective-permute-start.2 = (bf16[64,768]{1,0:T(8,128)(2,1)S(1)}, bf16[64,768]{1,0:T(8,128)(2,1)S(1)}, u32[]{:S(2)}, u32[]{:S(2)}) collective-permute-start(bf16[64,768]{1,0:T(8,128)(2,1)S(1)} %broadcast_select_fusion.5), channel_id=1, source_target_pairs={{0,1},{1,0},{2,3},{3,2},{4,5},{5,4},{6,7},{7,6},{8,9},{9,8},{10,11... | collective-permute-start | bytes 294920 | tf_op jit(solution)/shard_map/ppermute | solution.py:52
  28.5 4.9 %collective-permute-start.3 = (bf16[64,768]{1,0:T(8,128)(2,1)S(1)}, bf16[64,768]{1,0:T(8,128)(2,1)S(1)}, u32[]{:S(2)}, u32[]{:S(2)}) collective-permute-start(bf16[64,768]{1,0:T(8,128)(2,1)S(1)} %add_convert_fusion.1), channel_id=1, source_target_pairs={{0,2},{1,3},{2,0},{3,1},{4,6},{5,7},{6,4},{7,5},{8,10},{9,11},{10,... | collective-permute-start | bytes 294920 | tf_op jit(solution)/shard_map/ppermute | solution.py:52
  33.4 1.5 %collective-permute-start.4 = (f32[64,768]{1,0:T(8,128)S(1)}, f32[64,768]{1,0:T(8,128)S(1)}, u32[]{:S(2)}, u32[]{:S(2)}) collective-permute-start(f32[64,768]{1,0:T(8,128)S(1)} %convert_add_fusion.3), channel_id=1, source_target_pairs={{0,1},{1,0},{2,3},{3,2},{4,5},{5,4},{6,7},{7,6},{8,9},{9,8},{10,11... | collective-permute-start | bytes 589832 | tf_op jit(solution)/shard_map/ppermute | solution.py:52
  33.5 1.8 %copy-start.8 = (bf16[768,192]{0,1:T(8,128)(2,1)S(1)}, bf16[768,192]{0,1:T(8,128)(2,1)}, u32[]{:S(2)}) copy-start(bf16[768,192]{0,1:T(8,128)(2,1)} %param.23) | copy-start | bytes 884740
  33.5 1.8 %copy-start.10 = (f32[768]{0:T(1024)S(1)}, f32[768]{0:T(1024)}, u32[]{:S(2)}) copy-start(f32[768]{0:T(1024)} %param.18) | copy-start | bytes 9220
  35.8 1.0 %copy-start.3 = (bf16[192,768]{1,0:T(8,128)(2,1)S(1)}, bf16[192,768]{1,0:T(8,128)(2,1)}, u32[]{:S(2)}) copy-start(bf16[192,768]{1,0:T(8,128)(2,1)} %param.25) | copy-start | bytes 884740
  36.2 1.1 %copy-start.5 = (f32[2,64]{1,0:T(2,128)S(1)}, f32[2,64]{1,0:T(2,128)}, u32[]{:S(2)}) copy-start(f32[2,64]{1,0:T(2,128)} %param.16) | copy-start | bytes 1540
  37.0 1.4 %collective-permute-start.5 = (bf16[64,768]{1,0:T(8,128)(2,1)S(1)}, bf16[64,768]{1,0:T(8,128)(2,1)S(1)}, u32[]{:S(2)}, u32[]{:S(2)}) collective-permute-start(bf16[64,768]{1,0:T(8,128)(2,1)S(1)} %broadcast_select_fusion.2), channel_id=1, source_target_pairs={{0,1},{1,0},{2,3},{3,2},{4,5},{5,4},{6,7},{7,6},{8,9},{9,8},{10,11... | collective-permute-start | bytes 294920 | tf_op jit(solution)/shard_map/ppermute | solution.py:52
  38.4 4.9 %collective-permute-start.6 = (bf16[64,768]{1,0:T(8,128)(2,1)S(1)}, bf16[64,768]{1,0:T(8,128)(2,1)S(1)}, u32[]{:S(2)}, u32[]{:S(2)}) collective-permute-start(bf16[64,768]{1,0:T(8,128)(2,1)S(1)} %add_convert_fusion), channel_id=1, source_target_pairs={{0,2},{1,3},{2,0},{3,1},{4,6},{5,7},{6,4},{7,5},{8,10},{9,11},{10,... | collective-permute-start | bytes 294920 | tf_op jit(solution)/shard_map/ppermute | solution.py:52
  43.4 1.5 %collective-permute-start.7 = (f32[64,768]{1,0:T(8,128)S(1)}, f32[64,768]{1,0:T(8,128)S(1)}, u32[]{:S(2)}, u32[]{:S(2)}) collective-permute-start(f32[64,768]{1,0:T(8,128)S(1)} %convert_add_fusion.2), channel_id=1, source_target_pairs={{0,1},{1,0},{2,3},{3,2},{4,5},{5,4},{6,7},{7,6},{8,9},{9,8},{10,11... | collective-permute-start | bytes 589832 | tf_op jit(solution)/shard_map/ppermute | solution.py:52
  43.6 1.7 %copy-start.6 = (bf16[768,768]{1,0:T(8,128)(2,1)S(1)}, bf16[768,768]{1,0:T(8,128)(2,1)}, u32[]{:S(2)}) copy-start(bf16[768,768]{1,0:T(8,128)(2,1)} %param.26) | copy-start | bytes 3538948
  43.6 1.7 %copy-start.11 = (f32[768]{0:T(1024)S(1)}, f32[768]{0:T(1024)}, u32[]{:S(2)}) copy-start(f32[768]{0:T(1024)} %param.20) | copy-start | bytes 9220
  47.2 1.4 %collective-permute-start.8 = (bf16[128,2,192]{2,0,1:T(8,128)(2,1)S(1)}, bf16[128,2,192]{2,0,1:T(8,128)(2,1)S(1)}, u32[]{:S(2)}, u32[]{:S(2)}) collective-permute-start(bf16[128,2,192]{2,0,1:T(8,128)(2,1)S(1)} %select_bitcast_fusion.1), channel_id=1, source_target_pairs={{0,1},{1,0},{2,3},{3,2},{4,5},{5,4},{6,7},{7,6},{8,9},{9,8},{10,11... | collective-permute-start | bytes 294920 | tf_op jit(solution)/shard_map/ppermute | solution.py:52
  48.7 5.6 %collective-permute-start.9 = (f32[128,192]{1,0:T(8,128)S(1)}, f32[128,192]{1,0:T(8,128)S(1)}, u32[]{:S(2)}, u32[]{:S(2)}) collective-permute-start(f32[128,192]{1,0:T(8,128)S(1)} %select_bitcast_fusion), channel_id=1, source_target_pairs={{0,2},{1,3},{2,0},{3,1},{4,6},{5,7},{6,4},{7,5},{8,10},{9,11},{10,... | collective-permute-start | bytes 294920 | tf_op jit(solution)/shard_map/ppermute | solution.py:52
  55.0 5.8 %collective-permute-start.12 = (bf16[1,6272]{1,0:T(2,128)(2,1)S(1)}, bf16[1,6272]{1,0:T(2,128)(2,1)S(1)}, u32[]{:S(2)}, u32[]{:S(2)}) collective-permute-start(bf16[1,6272]{1,0:T(2,128)(2,1)S(1)} %get-tuple-element.21), channel_id=1, source_target_pairs={{0,12},{4,8},{8,4},{12,0},{1,13},{5,9},{9,5},{13,1},{2,14},{6,10},... | collective-permute-start | bytes 37640 | tf_op jit(solution)/shard_map/ppermute | solution.py:193
  58.8 4.7 %collective-permute-start.11 = (bf16[1,6272]{1,0:T(2,128)(2,1)S(1)}, bf16[1,6272]{1,0:T(2,128)(2,1)S(1)}, u32[]{:S(2)}, u32[]{:S(2)}) collective-permute-start(bf16[1,6272]{1,0:T(2,128)(2,1)S(1)} %get-tuple-element.22), channel_id=1, source_target_pairs={{0,8},{4,12},{8,0},{12,4},{1,9},{5,13},{9,1},{13,5},{2,10},{6,14},... | collective-permute-start | bytes 37640 | tf_op jit(solution)/shard_map/ppermute | solution.py:193
  58.8 4.7 %collective-permute-start.10 = (bf16[1,6272]{1,0:T(2,128)(2,1)S(1)}, bf16[1,6272]{1,0:T(2,128)(2,1)S(1)}, u32[]{:S(2)}, u32[]{:S(2)}) collective-permute-start(bf16[1,6272]{1,0:T(2,128)(2,1)S(1)} %get-tuple-element.23), channel_id=1, source_target_pairs={{0,4},{4,0},{8,12},{12,8},{1,5},{5,1},{9,13},{13,9},{2,6},{6,2},{1... | collective-permute-start | bytes 37640 | tf_op jit(solution)/shard_map/ppermute | solution.py:193
